TPU v7x, 32 devices: a whole 2x2x4 slice. The times are simulated.
32 devices in a mesh: groups: 2 (over y), sec: 4 (over x, core), plane: 4 (over z).
Axes of the slice: x: 2, y: 2, z: 4, core: 2. Of those that a mesh axis runs over, the one named last changes fastest.
Arguments:
- tokens: bfloat16 [16, 512, 1024], P(('groups', 'sec'), 'plane'), parts along dimension 0, may hold values from -8 to 8
- counts: int32 [16], P('groups'), parts along dimension 0, may hold values from 128 to 512, as said below
- region_ids: int32 [16, 512], P(('groups', 'sec'), 'plane'), parts along dimension 0, may hold values from 0 to 31
- norm_gains: float32 [2, 1024], replicated, may hold values from 0.1 to 1.9
- cross_qkv: bfloat16 [1024, 3072], P('plane'), may hold values from -2 to 2
- cross_out: bfloat16 [1024, 1024], P('plane'), may hold values from -0.1875 to 0.1875
- plane_qkv: bfloat16 [1024, 3072], P('plane'), may hold values from -2 to 2
- plane_out: bfloat16 [1024, 1024], P('plane'), may hold values from -0.1875 to 0.1875
Outputs:
- encoded: bfloat16 [16, 512, 1024], P(('groups', 'sec'), 'plane'), parts along dimension 0
- pooled: float32 [64, 1024], P(('groups', 'sec', 'plane')), parts along dimension 0
There are 2 independent parts, one for each index of `groups`. A program takes and returns all parts, laid end to end along the dimension named above; an argument that names none is the same for every part. Nothing has to cross between parts.
Inputs may be any that keep to these rules, and one draw needn't show every extreme that they name: `counts`: valid tissue tokens of each section; they are the first positions of the section.
All inputs are finite; a program needn't handle non-finite values.
Results may differ from a plain program's by a relative error of at most 0.009.
Values may be sent and summed in bfloat16 or wider, within the bound.
No kernel may reach another device: no remote copies, remote signals or barrier semaphores. Data moves between devices by JAX's collectives and lax.ppermute only.
A program may use at most 64 MiB of HBM per device.

v0:
```python
import math
import jax
import jax.numpy as jnp
from jax import lax
from jax.sharding import PartitionSpec as P

HEADS = 16
HEAD_DIM = 64
WINDOW = 128
negative_big = -1e30


def shifted_2(value, axis, by):
    peers = lax.axis_size(axis)
    pairs = [(i, i + by) for i in range(peers) if 0 <= i + by < peers]
    return lax.ppermute(value, axis, pairs)


def rms_norm(values, gain):
    wide = values.astype(jnp.float32)
    scaled = wide * lax.rsqrt(jnp.mean(wide * wide, axis=-1, keepdims=True) + 1e-06) * gain
    return scaled.astype(jnp.bfloat16)


def masked_softmax(scores, allowed):
    shifted = jnp.where(allowed, scores, negative_big)
    top = jnp.max(shifted, axis=-1, keepdims=True)
    expo = jnp.where(allowed, jnp.exp(shifted - top), 0.0)
    return (expo / jnp.sum(expo, axis=-1, keepdims=True)).astype(jnp.bfloat16)


def fold_product(inputs, weight_piece):
    return jnp.dot(inputs, weight_piece, preferred_element_type=jnp.float32)


def gather_pieces(shard):
    groups = lax.axis_size("groups")
    sections = lax.axis_size("sec")
    pair = 2 if sections % 2 == 0 else 1
    width = shard.shape[1] // (groups * pair)
    g = lax.axis_index("groups")
    k = lax.axis_index("sec") % pair
    own = g * pair + k
    mine = lax.dynamic_slice_in_dim(shard, own * width, width, axis=1)
    first = lax.all_gather(mine, "plane", axis=0, tiled=True)
    by_group = [(own, first)]
    for step in range(1, groups):
        moved = [(i, (i + step) % groups) for i in range(groups)]
        source = lax.rem(g - step + groups, groups)
        by_group.append((source * pair + k, lax.ppermute(first, "groups", moved)))
    held = list(by_group)
    if pair == 2:
        swap = [(i, i ^ 1) for i in range(sections)]
        for piece, block in by_group:
            held.append((piece - k + (1 - k), lax.ppermute(block, "sec", swap)))
    return (held, width)


def project(inputs, pieces):
    held, width = pieces
    out = jnp.zeros((inputs.shape[0], width * len(held)), jnp.float32)
    for piece, block in held:
        part = jnp.dot(inputs, block, preferred_element_type=jnp.float32)
        out = lax.dynamic_update_slice_in_dim(out, part, piece * width, axis=1)
    return out


def attend_items(pieces):
    packed_all, flags_all = pieces
    seq_len = packed_all.shape[2]
    block_len = 512
    score_scale = 1.0 / math.sqrt(HEAD_DIM)
    key_index = jnp.arange(seq_len, dtype=jnp.int32)

    def one_item(item_pair):
        packed, key_flag = item_pair
        key_rows = packed[:, HEAD_DIM : 2 * HEAD_DIM]
        value_rows = packed[:, 2 * HEAD_DIM :]
        key_alive = key_flag > 0.5
        query_blocks = packed[:, :HEAD_DIM].reshape(seq_len // block_len, block_len, HEAD_DIM)
        block_starts = jnp.arange(seq_len // block_len, dtype=jnp.int32) * block_len

        def one_block(block_pair):
            query_rows, offset = block_pair
            scores = (
                jnp.einsum("qd,kd->qk", query_rows, key_rows, preferred_element_type=jnp.float32)
                * score_scale
            )
            own_index = offset + jnp.arange(block_len, dtype=jnp.int32)
            allowed = key_alive[None, :] | (key_index[None, :] == own_index[:, None])
            attention = masked_softmax(scores, allowed)
            return jnp.dot(attention, value_rows, preferred_element_type=jnp.float32).astype(
                jnp.bfloat16
            )

        return lax.map(one_block, (query_blocks, block_starts)).reshape(seq_len, HEAD_DIM)

    return lax.map(one_item, (packed_all[0], flags_all[0]))[None]


def body(tokens, counts, region_ids, norm_gains, cross_qkv, cross_out, plane_qkv, plane_out):
    sec_block, tok_block, model_width = tokens.shape
    plane_count = lax.axis_size("plane")
    regions = 2 * lax.axis_size("sec") * plane_count
    positions = lax.axis_index("plane") * tok_block + jnp.arange(tok_block, dtype=jnp.int32)
    padded_counts = jnp.concatenate(
        [jnp.zeros((1,), jnp.int32), counts, jnp.zeros((1,), jnp.int32)]
    )
    near_counts = lax.dynamic_slice_in_dim(
        padded_counts, lax.axis_index("sec") * sec_block, sec_block + 2
    )
    near_valid = positions[None, :] < near_counts[:, None]
    own_valid = near_valid[1 : sec_block + 1]
    score_scale = 1.0 / math.sqrt(HEAD_DIM)
    cross_qkv_pieces = gather_pieces(cross_qkv)
    cross_out_pieces = gather_pieces(cross_out)
    plane_qkv_pieces = gather_pieces(plane_qkv)
    plane_out_pieces = gather_pieces(plane_out)
    normed = rms_norm(tokens, norm_gains[0])
    inputs = normed.reshape(-1, model_width)
    result = project(inputs, cross_qkv_pieces)
    projected = result.astype(jnp.bfloat16).reshape(sec_block, tok_block, 3 * model_width)
    own_kv = projected[:, :, model_width:]
    from_below = shifted_2(own_kv[sec_block - 1], "sec", 1)
    from_above = shifted_2(own_kv[0], "sec", -1)
    near_kv = jnp.concatenate([from_below[None], own_kv, from_above[None]], axis=0)
    queries = projected[:, :, :model_width]
    windows = tok_block // WINDOW
    query_win = queries.reshape(sec_block, windows, WINDOW, HEADS, HEAD_DIM)
    pair_win = near_kv.reshape(sec_block + 2, windows, WINDOW, 2, HEADS, HEAD_DIM)
    stacked = jnp.concatenate(
        [pair_win[0:sec_block], pair_win[1 : sec_block + 1], pair_win[2 : sec_block + 2]], axis=2
    )
    valid_win = near_valid.reshape(sec_block + 2, windows, WINDOW)
    valid_three = jnp.concatenate(
        [valid_win[0:sec_block], valid_win[1 : sec_block + 1], valid_win[2 : sec_block + 2]], axis=2
    )
    itself = jnp.arange(3 * WINDOW)[None, :] == jnp.arange(WINDOW)[:, None] + WINDOW
    scores = (
        jnp.einsum(
            "snqhd,snkhd->snhqk", query_win, stacked[:, :, :, 0], preferred_element_type=jnp.float32
        )
        * score_scale
    )
    allowed = valid_three[:, :, None, None, :] | itself[None, None, None]
    attention = masked_softmax(scores, allowed)
    context = jnp.einsum(
        "snhqk,snkhd->snqhd", attention, stacked[:, :, :, 1], preferred_element_type=jnp.float32
    )
    context = context.astype(jnp.bfloat16).reshape(-1, model_width)
    result = project(context, cross_out_pieces)
    after_cross = (tokens.reshape(-1, model_width).astype(jnp.float32) + result).astype(
        jnp.bfloat16
    )
    normed = rms_norm(after_cross, norm_gains[1])
    result = project(normed, plane_qkv_pieces)
    projected = result.astype(jnp.bfloat16).reshape(sec_block, tok_block, 3, HEADS, HEAD_DIM)
    per_device = sec_block * HEADS // plane_count
    heads_first = jnp.transpose(projected, (0, 3, 1, 2, 4)).reshape(
        plane_count, per_device, tok_block, 3 * HEAD_DIM
    )
    key_flags = jnp.broadcast_to(own_valid[:, None, :], (sec_block, HEADS, tok_block)).astype(
        jnp.bfloat16
    )
    key_flags = key_flags.reshape(plane_count, per_device, tok_block)
    attended = attend_items(
        (
            lax.all_to_all(heads_first, "plane", split_axis=0, concat_axis=2, tiled=True),
            lax.all_to_all(key_flags, "plane", split_axis=0, concat_axis=2, tiled=True),
        )
    )
    returned = lax.all_to_all(attended, "plane", split_axis=2, concat_axis=0, tiled=True)
    context = jnp.transpose(
        returned.reshape(sec_block, HEADS, tok_block, HEAD_DIM), (0, 2, 1, 3)
    ).reshape(-1, model_width)
    result = project(context, plane_out_pieces)
    encoded = (after_cross.astype(jnp.float32) + result).astype(jnp.bfloat16)
    labels = region_ids.reshape(-1)
    member = (jnp.arange(regions, dtype=jnp.int32)[:, None] == labels[None, :]) & own_valid.reshape(
        -1
    )[None, :]
    region_sum = jnp.dot(member.astype(jnp.bfloat16), encoded, preferred_element_type=jnp.float32)
    region_count = jnp.sum(member.astype(jnp.float32), axis=1)
    totals, counted = (
        lax.psum_scatter(region_sum, ("sec", "plane"), scatter_dimension=0, tiled=True),
        lax.psum_scatter(region_count, ("sec", "plane"), scatter_dimension=0, tiled=True),
    )
    pooled = totals / jnp.maximum(counted, 1.0)[:, None]
    return (encoded.reshape(sec_block, tok_block, model_width), pooled)


def solution(mesh):
    in_specs = (
        P(("groups", "sec"), "plane", None),
        P("groups"),
        P(("groups", "sec"), "plane"),
        P(),
        P("plane", None),
        P("plane", None),
        P("plane", None),
        P("plane", None),
    )
    out_specs = (P(("groups", "sec"), "plane", None), P(("groups", "sec", "plane"), None))
    return jax.shard_map(body, mesh=mesh, in_specs=in_specs, out_specs=out_specs, check_vma=False)
```

profile of v0, /device:TPU:8, one launch (start us, length us, event | category | flops | bytes accessed | tf_op | source)
XLA Modules:
  0.0 392.4 jit_solution(481135209715958584)
XLA Ops:
  11.2 35.6 %all-gather.3.cloned.1.call-done = bf16[1024,768]{1,0:T(8,128)(2,1)} async-done(((bf16[256,768]{1,0:T(8,128)(2,1)}), bf16[1024,768]{1,0:T(8,128)(2,1)}) %all-gather.3.cloned.1.call-update) | async-done | bytes 1572880 | tf_op jit(solution)/shard_map/all_gather | solution.py:45
  49.2 18.7 %all_gather.13 = bf16[1024,256]{1,0:T(8,128)(2,1)} all-gather(bf16[256,256]{1,0:T(8,128)(2,1)S(1)} %constant_dynamic-slice_fusion.2), channel_id=1, replica_groups=mesh['groups'=2,'sec'=4,'plane'=4] {'plane'}, dimensions={0}, use_global_device_ids=true | all-gather | bytes 655360 | tf_op jit(solution)/shard_map/all_gather | solution.py:45
  69.2 15.3 %collective-permute-done = bf16[1024,768]{1,0:T(8,128)(2,1)} collective-permute-done((bf16[1024,768]{1,0:T(8,128)(2,1)}, bf16[1024,768]{1,0:T(8,128)(2,1)}, u32[]{:S(2)}, u32[]{:S(2)}) %collective-permute-start) | collective-permute-done | bytes 1572896 | tf_op jit(solution)/shard_map/ppermute | solution.py:50
  84.7 3.6 all-gather.5.cloned.1.call-done
  89.8 2.0 convolution_dynamic-update-slice_fusion.7
  91.8 2.0 convolution_dynamic-update-slice_fusion.6
  95.8 2.0 convolution_dynamic-update-slice_fusion.4
  98.9 2.5 collective-permute-start.3
  107.7 20.3 %collective-permute-done.8 = bf16[1024,768]{1,0:T(8,128)(2,1)} collective-permute-done((bf16[1024,768]{1,0:T(8,128)(2,1)}, bf16[1024,768]{1,0:T(8,128)(2,1)}, u32[]{:S(2)}, u32[]{:S(2)}) %collective-permute-start.8) | collective-permute-done | bytes 1572896 | tf_op jit(solution)/shard_map/ppermute | solution.py:50
  128.5 2.7 pad_maximum_fusion.2
  131.3 2.4 copy.53
  135.0 2.0 pad_maximum_fusion
  138.0 3.2 fusion.56
  151.6 2.0 convolution_dynamic-update-slice_fusion.2
  153.7 2.0 convolution_dynamic-update-slice_fusion.1
  155.8 2.0 convolution_dynamic-update-slice_fusion
  159.3 39.7 %all_to_all.45 = bf16[4,8,128,192]{2,3,1,0:T(8,128)(2,1)S(1)} all-to-all(bf16[4,8,128,192]{2,3,1,0:T(8,128)(2,1)S(1)} %bitcast.141), channel_id=1, replica_groups=mesh['groups'=2,'sec'=4,'plane'=4] {'plane'}, dimensions={0} | all-to-all | bytes 3145728 | tf_op jit(solution)/shard_map/all_to_all | solution.py:168
  199.7 5.0 %all-to-all-start = ((bf16[4,8,128]{2,1,0:T(8,128)(2,1)}), bf16[4,8,128]{2,1,0:T(8,128)(2,1)S(1)}, u32[]{:S(2)}, u32[]{:S(2)}) async-start(bf16[4,8,128]{2,1,0:T(8,128)(2,1)} %broadcast_in_dim.86), calls=%async_computation | async-start | bytes 16384 | tf_op jit(solution)/shard_map/all_to_all | solution.py:169
  204.7 2.6 copy.68
  208.9 16.5 %while.11 = (s32[]{:T(128)}, bf16[8,512,64]{1,2,0:T(8,128)(2,1)S(1)}, bf16[8,512]{1,0:T(8,128)(2,1)S(1)}, bf16[8,512,192]{2,1,0:T(8,128)(2,1)}, s32[]{:T(128)}) while((s32[]{:T(128)}, bf16[8,512,64]{1,2,0:T(8,128)(2,1)S(1)}, bf16[8,512]{1,0:T(8,128)(2,1)S(1)}, bf16[8,512,192]{2,1,0:T(8,128)(2,1)}, s32[]{:T(128)}) %tuple.52), condition=%wide.region_7.8_spmd.clone, body=%wide.region_4.7_spmd.clone.sunk | while | flops 71336448 | bytes 3945545 | solution.py:98
  227.8 4.8 %all-to-all-start.2 = ((bf16[4,2,32768]{2,1,0:T(2,128)(2,1)}), bf16[4,2,32768]{2,1,0:T(2,128)(2,1)S(1)}, u32[]{:S(2)}, u32[]{:S(2)}) async-start(bf16[4,2,32768]{2,1,0:T(2,128)(2,1)} %reshape.161), calls=%async_computation.2 | async-start | bytes 1048576 | tf_op jit(solution)/shard_map/all_to_all | solution.py:172
  233.5 21.6 %all_gather.15 = bf16[1024,256]{1,0:T(8,128)(2,1)S(1)} all-gather(bf16[256,256]{1,0:T(8,128)(2,1)S(1)} %constant_dynamic-slice_fusion), channel_id=1, replica_groups=mesh['groups'=2,'sec'=4,'plane'=4] {'plane'}, dimensions={0}, use_global_device_ids=true | all-gather | bytes 655360 | tf_op jit(solution)/shard_map/all_gather | solution.py:45
  258.0 30.8 %all-reduce.1 = f32[32]{0:T(128)S(1)} all-reduce(f32[32]{0:T(128)S(1)} %convert_reduce_fusion), channel_id=3, replica_groups=mesh['groups'=2,'sec'=4,'plane'=4] {'sec','plane'}, use_global_device_ids=true, to_apply=%region_10.11.clone | all-reduce | flops 32 | bytes 256
  295.0 89.5 %all-reduce.4.cloned.1.call-done = f32[32,1024]{1,0:T(8,128)} async-done(((f32[32,1024]{1,0:T(8,128)}), f32[32,1024]{1,0:T(8,128)}) %all-reduce.4.cloned.1.call-update) | async-done | bytes 131088
  (158 shorter events, 64.7 us)
Async XLA Ops:
  7.2 39.7 %all-gather.3.cloned.1.call-start = ((), (), s32[]{:S(2)}) async-start(), calls=%async_computation.3 | async-start | bytes 1966080 | tf_op jit(solution)/shard_map/all_gather | solution.py:45
  8.6 59.7 %copy-start.10 = (s32[8]{0:T(128)S(1)}, s32[8]{0:T(128)}, u32[]{:S(2)}) copy-start(s32[8]{0:T(128)} %param.11) | copy-start | bytes 100
  8.6 60.5 %copy-start.2 = (bf16[2,128,1024]{2,1,0:T(8,128)(2,1)S(1)}, bf16[2,128,1024]{2,1,0:T(8,128)(2,1)}, u32[]{:S(2)}) copy-start(bf16[2,128,1024]{2,1,0:T(8,128)(2,1)} %param.10) | copy-start | bytes 1572868
  9.4 75.1 %copy-start.7 = (f32[2,1024]{1,0:T(2,128)S(1)}, f32[2,1024]{1,0:T(2,128)}, u32[]{:S(2)}) copy-start(f32[2,1024]{1,0:T(2,128)} %param.13) | copy-start | bytes 24580
  9.4 78.9 %all-gather.5.cloned.1.call-start = ((), (), s32[]{:S(2)}) async-start(), calls=%async_computation.4 | async-start | bytes 1966080 | tf_op jit(solution)/shard_map/all_gather | solution.py:45
  46.9 37.6 %collective-permute-start = (bf16[1024,768]{1,0:T(8,128)(2,1)}, bf16[1024,768]{1,0:T(8,128)(2,1)}, u32[]{:S(2)}, u32[]{:S(2)}) collective-permute-start(bf16[1024,768]{1,0:T(8,128)(2,1)} %all-gather.3.cloned.1.call-done), channel_id=1, source_target_pairs={{0,16},{16,0},{1,17},{17,1},{2,18},{18,2},{3,19},{19,3},{4,20},{20... | collective-permute-start | bytes 4718600 | tf_op jit(solution)/shard_map/ppermute | solution.py:50
  67.9 35.1 %collective-permute-start.5 = (bf16[1024,256]{1,0:T(8,128)(2,1)}, bf16[1024,256]{1,0:T(8,128)(2,1)}, u32[]{:S(2)}, u32[]{:S(2)}) collective-permute-start(bf16[1024,256]{1,0:T(8,128)(2,1)} %all_gather.13), channel_id=1, source_target_pairs={{0,16},{16,0},{1,17},{17,1},{2,18},{18,2},{3,19},{19,3},{4,20},{20... | collective-permute-start | bytes 1572872 | tf_op jit(solution)/shard_map/ppermute | solution.py:50
  68.3 78.3 %collective-permute-start.6 = (bf16[1024,256]{1,0:T(8,128)(2,1)}, bf16[1024,256]{1,0:T(8,128)(2,1)}, u32[]{:S(2)}, u32[]{:S(2)}) collective-permute-start(bf16[1024,256]{1,0:T(8,128)(2,1)} %all_gather.13), channel_id=1, source_target_pairs={{0,4},{4,0},{8,12},{12,8},{1,5},{5,1},{9,13},{13,9},{2,6},{6,2},{1... | collective-permute-start | bytes 1572872 | tf_op jit(solution)/shard_map/ppermute | solution.py:55
  68.5 25.3 %collective-permute-start.1 = (bf16[1024,768]{1,0:T(8,128)(2,1)}, bf16[1024,768]{1,0:T(8,128)(2,1)}, u32[]{:S(2)}, u32[]{:S(2)}) collective-permute-start(bf16[1024,768]{1,0:T(8,128)(2,1)} %all-gather.3.cloned.1.call-done), channel_id=1, source_target_pairs={{0,4},{4,0},{8,12},{12,8},{1,5},{5,1},{9,13},{13,9},{2,6},{6,2},{1... | collective-permute-start | bytes 4718600 | tf_op jit(solution)/shard_map/ppermute | solution.py:55
  84.5 11.3 %collective-permute-start.2 = (bf16[1024,768]{1,0:T(8,128)(2,1)}, bf16[1024,768]{1,0:T(8,128)(2,1)}, u32[]{:S(2)}, u32[]{:S(2)}) collective-permute-start(bf16[1024,768]{1,0:T(8,128)(2,1)} %collective-permute-done), channel_id=1, source_target_pairs={{0,4},{4,0},{8,12},{12,8},{1,5},{5,1},{9,13},{13,9},{2,6},{6,2},{1... | collective-permute-start | bytes 4718600 | tf_op jit(solution)/shard_map/ppermute | solution.py:55
  88.3 39.8 %collective-permute-start.8 = (bf16[1024,768]{1,0:T(8,128)(2,1)}, bf16[1024,768]{1,0:T(8,128)(2,1)}, u32[]{:S(2)}, u32[]{:S(2)}) collective-permute-start(bf16[1024,768]{1,0:T(8,128)(2,1)} %all-gather.5.cloned.1.call-done), channel_id=1, source_target_pairs={{0,16},{16,0},{1,17},{17,1},{2,18},{18,2},{3,19},{19,3},{4,20},{20... | collective-permute-start | bytes 4718600 | tf_op jit(solution)/shard_map/ppermute | solution.py:50
  98.9 29.1 %collective-permute-start.3 = (bf16[128,2048]{1,0:T(8,128)(2,1)}, bf16[128,2048]{1,0:T(8,128)(2,1)}, u32[]{:S(2)}, u32[]{:S(2)}) collective-permute-start(bf16[128,2048]{1,0:T(8,128)(2,1)} %get-tuple-element.85), channel_id=1, source_target_pairs={{0,4},{4,8},{8,12},{1,5},{5,9},{9,13},{2,6},{6,10},{10,14},{3,7},{... | collective-permute-start | bytes 1572872 | tf_op jit(solution)/shard_map/ppermute | solution.py:16
  101.4 27.1 %collective-permute-start.4 = (bf16[128,2048]{1,0:T(8,128)(2,1)}, bf16[128,2048]{1,0:T(8,128)(2,1)}, u32[]{:S(2)}, u32[]{:S(2)}) collective-permute-start(bf16[128,2048]{1,0:T(8,128)(2,1)} %get-tuple-element.86), channel_id=1, source_target_pairs={{4,0},{8,4},{12,8},{5,1},{9,5},{13,9},{6,2},{10,6},{14,10},{7,3},{... | collective-permute-start | bytes 1572872 | tf_op jit(solution)/shard_map/ppermute | solution.py:16
  103.1 44.9 %collective-permute-start.7 = (bf16[1024,256]{1,0:T(8,128)(2,1)}, bf16[1024,256]{1,0:T(8,128)(2,1)}, u32[]{:S(2)}, u32[]{:S(2)}) collective-permute-start(bf16[1024,256]{1,0:T(8,128)(2,1)} %collective-permute-done.5), channel_id=1, source_target_pairs={{0,4},{4,0},{8,12},{12,8},{1,5},{5,1},{9,13},{13,9},{2,6},{6,2},{1... | collective-permute-start | bytes 1572872 | tf_op jit(solution)/shard_map/ppermute | solution.py:55
  128.0 25.7 %collective-permute-start.9 = (bf16[1024,768]{1,0:T(8,128)(2,1)}, bf16[1024,768]{1,0:T(8,128)(2,1)}, u32[]{:S(2)}, u32[]{:S(2)}) collective-permute-start(bf16[1024,768]{1,0:T(8,128)(2,1)} %all-gather.5.cloned.1.call-done), channel_id=1, source_target_pairs={{0,4},{4,0},{8,12},{12,8},{1,5},{5,1},{9,13},{13,9},{2,6},{6,2},{1... | collective-permute-start | bytes 4718600 | tf_op jit(solution)/shard_map/ppermute | solution.py:55
  128.0 27.7 %collective-permute-start.10 = (bf16[1024,768]{1,0:T(8,128)(2,1)}, bf16[1024,768]{1,0:T(8,128)(2,1)}, u32[]{:S(2)}, u32[]{:S(2)}) collective-permute-start(bf16[1024,768]{1,0:T(8,128)(2,1)} %collective-permute-done.8), channel_id=1, source_target_pairs={{0,4},{4,0},{8,12},{12,8},{1,5},{5,1},{9,13},{13,9},{2,6},{6,2},{1... | collective-permute-start | bytes 4718600 | tf_op jit(solution)/shard_map/ppermute | solution.py:55
  199.7 9.2 %all-to-all-start = ((bf16[4,8,128]{2,1,0:T(8,128)(2,1)}), bf16[4,8,128]{2,1,0:T(8,128)(2,1)S(1)}, u32[]{:S(2)}, u32[]{:S(2)}) async-start(bf16[4,8,128]{2,1,0:T(8,128)(2,1)} %broadcast_in_dim.86), calls=%async_computation | async-start | bytes 16384 | tf_op jit(solution)/shard_map/all_to_all | solution.py:169
  227.8 61.1 %all-to-all-start.2 = ((bf16[4,2,32768]{2,1,0:T(2,128)(2,1)}), bf16[4,2,32768]{2,1,0:T(2,128)(2,1)S(1)}, u32[]{:S(2)}, u32[]{:S(2)}) async-start(bf16[4,2,32768]{2,1,0:T(2,128)(2,1)} %reshape.161), calls=%async_computation.2 | async-start | bytes 1048576 | tf_op jit(solution)/shard_map/all_to_all | solution.py:172
  232.6 151.8 %all-reduce.4.cloned.1.call-start = ((), (), s32[]{:S(2)}) async-start(), calls=%async_computation.5 | async-start | bytes 262144
  255.2 33.7 %collective-permute-start.11 = (bf16[1024,256]{1,0:T(8,128)(2,1)S(1)}, bf16[1024,256]{1,0:T(8,128)(2,1)S(1)}, u32[]{:S(2)}, u32[]{:S(2)}) collective-permute-start(bf16[1024,256]{1,0:T(8,128)(2,1)S(1)} %all_gather.15), channel_id=1, source_target_pairs={{0,16},{16,0},{1,17},{17,1},{2,18},{18,2},{3,19},{19,3},{4,20},{20... | collective-permute-start | bytes 1572872 | tf_op jit(solution)/shard_map/ppermute | solution.py:50
  256.6 35.4 %collective-permute-start.12 = (bf16[1024,256]{1,0:T(8,128)(2,1)S(1)}, bf16[1024,256]{1,0:T(8,128)(2,1)}, u32[]{:S(2)}, u32[]{:S(2)}) collective-permute-start(bf16[1024,256]{1,0:T(8,128)(2,1)S(1)} %all_gather.15), channel_id=1, source_target_pairs={{0,4},{4,0},{8,12},{12,8},{1,5},{5,1},{9,13},{13,9},{2,6},{6,2},{1... | collective-permute-start | bytes 1572872 | tf_op jit(solution)/shard_map/ppermute | solution.py:55
  288.9 4.7 %collective-permute-start.13 = (bf16[1024,256]{1,0:T(8,128)(2,1)S(1)}, bf16[1024,256]{1,0:T(8,128)(2,1)S(1)}, u32[]{:S(2)}, u32[]{:S(2)}) collective-permute-start(bf16[1024,256]{1,0:T(8,128)(2,1)S(1)} %collective-permute-done.11), channel_id=1, source_target_pairs={{0,4},{4,0},{8,12},{12,8},{1,5},{5,1},{9,13},{13,9},{2,6},{6,2},{1... | collective-permute-start | bytes 1572872 | tf_op jit(solution)/shard_map/ppermute | solution.py:55
  293.5 92.4 %copy-start.1 = (bf16[256,3072]{1,0:T(8,128)(2,1)S(1)}, bf16[256,3072]{1,0:T(8,128)(2,1)}, u32[]{:S(2)}) copy-start(bf16[256,3072]{1,0:T(8,128)(2,1)} %param.14) | copy-start | bytes 4718596
  294.0 91.9 %copy-start.4 = (bf16[256,1024]{1,0:T(8,128)(2,1)}, bf16[256,1024]{1,0:T(8,128)(2,1)S(1)}, u32[]{:S(2)}) copy-start(bf16[256,1024]{1,0:T(8,128)(2,1)S(1)} %fusion.24) | copy-start | bytes 1572868
  (7 other events, 74.3 us)
Sparse Core Ops, SparseCore 0:
  9.6 37.2 all-gather.2
  49.0 39.2 all-gather.4
  295.0 89.3 all-reduce.3
where the time goes:
time: 394 us; the launch traced here: 392 us
  waiting for transfers between devices  166 us (42%)
  blocking collectives  111 us (28%)
  local copies, waits for them, and re-layouts  33.4 us (8%)
  matrix products  32.7 us (8%)
  starting transfers between devices  21.3 us (5%)
  between operations  15 us (4%)
  other arithmetic  12.9 us (3%)
    unnamed x4, waiting for transfers between devices  89.5 us
    all_gather x2, blocking collectives, gather_pieces(): first = lax.all_gather(mine, 'plane', axis=0, tiled=True)  40.4 us
    all_to_all x1, blocking collectives, body(): lax.all_to_all(heads_first, 'plane', split_axis=0, concat_axis=2, tiled=T...  39.7 us
    all_gather x2, waiting for transfers between devices, gather_pieces(): first = lax.all_gather(mine, 'plane', axis=0, tiled=True)  39.2 us
    ppermute x4, waiting for transfers between devices, gather_pieces(): by_group.append((source * pair + k, lax.ppermute(first, 'groups', moved)))  35.6 us
    unnamed x1, blocking collectives  30.8 us
    dot_general x16, matrix products, project(): part = jnp.dot(inputs, block, preferred_element_type=jnp.float32)  22.8 us
    unnamed x29, local copies, waits for them, and re-layouts  8.08 us
  transfers between devices with their start and end apart: 19, of which 6 were waited for; matrix products, arithmetic and copies ran while one was open for 13% of the time, Pallas kernels for 0%

commit v1 on v0

--- a/solution.py
+++ b/solution.py
@@ -3,6 +3,7 @@
 import jax.numpy as jnp
 from jax import lax
 from jax.sharding import PartitionSpec as P
+from jax.lax import axis_index, axis_size, ppermute
 
 HEADS = 16
 HEAD_DIM = 64
@@ -42,7 +43,23 @@
     k = lax.axis_index("sec") % pair
     own = g * pair + k
     mine = lax.dynamic_slice_in_dim(shard, own * width, width, axis=1)
-    first = lax.all_gather(mine, "plane", axis=0, tiled=True)
+
+    def follow_terms_on(t0, link_axis="plane"):
+        stack_in = []
+        n_shards = axis_size(link_axis)
+        for c in range(1, n_shards):
+            stack_in.append((c - 1, c))
+        found_now = stack_in + [(n_shards - 1, 0)]
+        next_value = t0
+        kept_rows = [next_value]
+        for _ in range(n_shards - 1):
+            next_value = ppermute(next_value, link_axis, found_now)
+            kept_rows += [next_value]
+        all_rows = jnp.concatenate([*reversed(kept_rows)], axis=0)
+        z2 = axis_index(link_axis)
+        return jnp.roll(all_rows, (z2 + 1) * next_value.shape[0], axis=0)
+
+    first = follow_terms_on(mine)
     by_group = [(own, first)]
     for step in range(1, groups):
         moved = [(i, (i + step) % groups) for i in range(groups)]

time: 394 us -> 402 us (1.020); the launches traced: 392 us -> 396 us
  blocking collectives: 111 us -> 30.6 us
  waiting for transfers between devices: 166 us -> 199 us
  other arithmetic: 12.9 us -> 42.8 us
  starting transfers between devices: 21.3 us -> 45.8 us
    ppermute x0 -> x12, waiting for transfers between devices: none -> 82.2 us  [follow_terms_on(): next_value = ppermute(next_value, link_axis, found_now)]
    all_gather x2 -> x0, blocking collectives: 40.4 us -> none  [gather_pieces(): first = lax.all_gather(mine, 'plane', axis=0, tiled=True)]
    all_to_all x1 -> x0, blocking collectives: 39.7 us -> none  [body(): lax.all_to_all(heads_first, 'plane', split_axis=0, concat_axis=2, tiled=T...]
    all_gather x2 -> x0, waiting for transfers between devices: 39.2 us -> none  [gather_pieces(): first = lax.all_gather(mine, 'plane', axis=0, tiled=True)]
    concatenate x0 -> x4, other arithmetic: none -> 29 us  [follow_terms_on(): return jnp.roll(all_rows, (z2 + 1) * next_value.shape[0], axis=0)]
    ppermute x0 -> x12, starting transfers between devices: none -> 17.2 us  [follow_terms_on(): next_value = ppermute(next_value, link_axis, found_now)]
    ppermute x4, waiting for transfers between devices: 35.6 us -> 26.7 us  [gather_pieces(): by_group.append((source * pair + k, lax.ppermute(first, 'groups', moved)))]
    all_to_all x0 -> x1, starting transfers between devices: none -> 6.91 us  [body(): lax.all_to_all(heads_first, 'plane', split_axis=0, concat_axis=2, tiled=T...]
  transfers between devices with their start and end apart: 19 -> 30, of which waited for: 6 -> 9; matrix products, arithmetic and copies ran while one was open for 13% -> 24% of each run, Pallas kernels for 0% -> 0%
where the time goes in v1:
time: 402 us; the launch traced here: 396 us
  waiting for transfers between devices  199 us (50%)
  starting transfers between devices  45.8 us (11%)
  other arithmetic  42.8 us (11%)
  matrix products  31.4 us (8%)
  local copies, waits for them, and re-layouts  30.6 us (8%)
  blocking collectives  30.6 us (8%)
  between operations  15.5 us (4%)
    unnamed x2, waiting for transfers between devices  90.1 us
    ppermute x12, waiting for transfers between devices, follow_terms_on(): next_value = ppermute(next_value, link_axis, found_now)  82.2 us
    unnamed x1, blocking collectives  30.6 us
    concatenate x4, other arithmetic, follow_terms_on(): return jnp.roll(all_rows, (z2 + 1) * next_value.shape[0], axis=0)  29 us
    ppermute x4, waiting for transfers between devices, gather_pieces(): by_group.append((source * pair + k, lax.ppermute(first, 'groups', moved)))  26.7 us
    dot_general x16, matrix products, project(): part = jnp.dot(inputs, block, preferred_element_type=jnp.float32)  21.4 us
    ppermute x12, starting transfers between devices, follow_terms_on(): next_value = ppermute(next_value, link_axis, found_now)  17.2 us
  transfers between devices with their start and end apart: 30, of which 9 were waited for; matrix products, arithmetic and copies ran while one was open for 24% of the time, Pallas kernels for 0%

profile of v1, /device:TPU:8, one launch (start us, length us, event | category | flops | bytes accessed | tf_op | source)
XLA Modules:
  0.0 396.0 jit_solution(7779436592615785248)
XLA Ops:
  10.2 9.3 %collective-permute-done = bf16[256,768]{1,0:T(8,128)(2,1)S(1)} collective-permute-done((bf16[256,768]{1,0:T(8,128)(2,1)S(1)}, bf16[256,768]{1,0:T(8,128)(2,1)S(1)}, u32[]{:S(2)}, u32[]{:S(2)}) %collective-permute-start) | collective-permute-done | bytes 393248 | tf_op jit(solution)/shard_map/ppermute | solution.py:56
  21.1 9.3 %collective-permute-done.1 = bf16[256,768]{1,0:T(8,128)(2,1)S(1)} collective-permute-done((bf16[256,768]{1,0:T(8,128)(2,1)S(1)}, bf16[256,768]{1,0:T(8,128)(2,1)S(1)}, u32[]{:S(2)}, u32[]{:S(2)}) %collective-permute-start.1) | collective-permute-done | bytes 393248 | tf_op jit(solution)/shard_map/ppermute | solution.py:56
  33.6 9.4 %collective-permute-done.2 = bf16[256,768]{1,0:T(8,128)(2,1)} collective-permute-done((bf16[256,768]{1,0:T(8,128)(2,1)S(1)}, bf16[256,768]{1,0:T(8,128)(2,1)}, u32[]{:S(2)}, u32[]{:S(2)}) %collective-permute-start.2) | collective-permute-done | bytes 393248 | tf_op jit(solution)/shard_map/ppermute | solution.py:56
  43.1 10.2 %fusion.28 = bf16[1024,768]{1,0:T(8,128)(2,1)S(1)} fusion(s32[]{:T(128)S(6)} %select_n.105, bf16[256,768]{1,0:T(8,128)(2,1)} %collective-permute-done.2, bf16[256,768]{1,0:T(8,128)(2,1)S(1)} %collective-permute-done.1, bf16[256,768]{1,0:T(8,128)(2,1)S(1)} %collective-permute-done, bf16[256,768]{1,0:T(8,128)(2,1)S(1)} %constant_dynamic-slice_fusion.3), kind=kLoop, calls=%fused_computation.54 | loop fusion | flops 12582912 | bytes 3145732 | tf_op jit(solution)/shard_map/jit(_roll_dynamic)/concatenate | solution.py:60
  55.9 9.8 %collective-permute-done.14 = bf16[256,768]{1,0:T(8,128)(2,1)S(1)} collective-permute-done((bf16[256,768]{1,0:T(8,128)(2,1)S(1)}, bf16[256,768]{1,0:T(8,128)(2,1)S(1)}, u32[]{:S(2)}, u32[]{:S(2)}) %collective-permute-start.14) | collective-permute-done | bytes 393248 | tf_op jit(solution)/shard_map/ppermute | solution.py:56
  65.8 2.7 collective-permute-start.9
  68.6 10.0 %collective-permute-done.9 = bf16[256,256]{1,0:T(8,128)(2,1)} collective-permute-done((bf16[256,256]{1,0:T(8,128)(2,1)}, bf16[256,256]{1,0:T(8,128)(2,1)}, u32[]{:S(2)}, u32[]{:S(2)}) %collective-permute-start.9) | collective-permute-done | bytes 131104 | tf_op jit(solution)/shard_map/ppermute | solution.py:56
  78.7 3.2 collective-permute-start.16
  82.4 3.7 collective-permute-done.3
  86.8 4.3 %fusion.50 = bf16[1024,256]{1,0:T(8,128)(2,1)} fusion(s32[]{:T(128)S(6)} %select_n.105, bf16[256,256]{1,0:T(8,128)(2,1)} %collective-permute-done.10, bf16[256,256]{1,0:T(8,128)(2,1)} %collective-permute-done.9, bf16[256,256]{1,0:T(8,128)(2,1)} %collective-permute-done.8, bf16[256,256]{1,0:T(8,128)(2,1)S(1)} %constant_dynamic-slice_fusion.2), kind=kLoop, calls=%fused_computation.118 | loop fusion | flops 4194304 | bytes 1048580 | tf_op jit(solution)/shard_map/jit(_roll_dynamic)/concatenate | solution.py:60
  91.8 9.8 %fusion.21 = bf16[1024,768]{1,0:T(8,128)(2,1)} fusion(s32[]{:T(128)S(6)} %select_n.105, bf16[256,768]{1,0:T(8,128)(2,1)} %collective-permute-done.16, bf16[256,768]{1,0:T(8,128)(2,1)} %collective-permute-done.15, bf16[256,768]{1,0:T(8,128)(2,1)S(1)} %collective-permute-done.14, bf16[256,768]{1,0:T(8,128)(2,1)S(1)} %constant_dynamic-slice_fusion.1), kind=kLoop, calls=%fused_computation.47 | loop fusion | flops 12582912 | bytes 3145732 | tf_op jit(solution)/shard_map/jit(_roll_dynamic)/concatenate | solution.py:60
  109.1 2.7 collective-permute-start.6
  116.4 23.0 %collective-permute-done.17 = bf16[1024,768]{1,0:T(8,128)(2,1)} collective-permute-done((bf16[1024,768]{1,0:T(8,128)(2,1)}, bf16[1024,768]{1,0:T(8,128)(2,1)}, u32[]{:S(2)}, u32[]{:S(2)}) %collective-permute-start.17) | collective-permute-done | bytes 1572896 | tf_op jit(solution)/shard_map/ppermute | solution.py:67
  149.1 3.2 fusion.84
  171.9 6.9 %all-to-all-start.1 = ((bf16[4,8,128,192]{2,3,1,0:T(8,128)(2,1)}), bf16[4,8,128,192]{2,3,1,0:T(8,128)(2,1)S(1)}, u32[]{:S(2)}, u32[]{:S(2)}) async-start(bf16[4,8,128,192]{2,3,1,0:T(8,128)(2,1)} %bitcast.26), calls=%async_computation.1 | async-start | bytes 3145728 | tf_op jit(solution)/shard_map/all_to_all | solution.py:185
  181.2 34.4 %collective-permute-done.20 = bf16[256,256]{1,0:T(8,128)(2,1)S(1)} collective-permute-done((bf16[256,256]{1,0:T(8,128)(2,1)S(1)}, bf16[256,256]{1,0:T(8,128)(2,1)S(1)}, u32[]{:S(2)}, u32[]{:S(2)}) %collective-permute-start.20) | collective-permute-done | bytes 131104 | tf_op jit(solution)/shard_map/ppermute | solution.py:56
  215.6 2.5 collective-permute-start.21
  218.7 6.9 %all-to-all-start = ((bf16[4,8,128]{2,1,0:T(8,128)(2,1)}), bf16[4,8,128]{2,1,0:T(8,128)(2,1)S(1)}, u32[]{:S(2)}, u32[]{:S(2)}) async-start(bf16[4,8,128]{2,1,0:T(8,128)(2,1)} %broadcast_in_dim.86), calls=%async_computation | async-start | bytes 16384 | tf_op jit(solution)/shard_map/all_to_all | solution.py:186
  227.3 2.6 copy.68
  229.9 16.5 %while.11 = (s32[]{:T(128)}, bf16[8,512,64]{1,2,0:T(8,128)(2,1)S(1)}, bf16[8,512]{1,0:T(8,128)(2,1)S(1)}, bf16[8,512,192]{2,1,0:T(8,128)(2,1)}, s32[]{:T(128)}) while((s32[]{:T(128)}, bf16[8,512,64]{1,2,0:T(8,128)(2,1)S(1)}, bf16[8,512]{1,0:T(8,128)(2,1)S(1)}, bf16[8,512,192]{2,1,0:T(8,128)(2,1)}, s32[]{:T(128)}) %tuple.50), condition=%wide.region_7.10_spmd.clone, body=%wide.region_4.9_spmd.clone.sunk | while | flops 71336448 | bytes 3945545 | solution.py:115
  248.8 4.8 %all-to-all-start.2 = ((bf16[4,2,32768]{2,1,0:T(2,128)(2,1)}), bf16[4,2,32768]{2,1,0:T(2,128)(2,1)S(1)}, u32[]{:S(2)}, u32[]{:S(2)}) async-start(bf16[4,2,32768]{2,1,0:T(2,128)(2,1)} %reshape.161), calls=%async_computation.2 | async-start | bytes 1048576 | tf_op jit(solution)/shard_map/all_to_all | solution.py:189
  253.6 4.8 %fusion.43 = bf16[1024,256]{1,0:T(8,128)(2,1)S(1)} fusion(s32[]{:T(128)S(6)} %select_n.105, bf16[256,256]{1,0:T(8,128)(2,1)S(1)} %collective-permute-done.22, bf16[256,256]{1,0:T(8,128)(2,1)S(1)} %collective-permute-done.21, bf16[256,256]{1,0:T(8,128)(2,1)S(1)} %collective-permute-done.20, bf16[256,256]{1,0:T(8,128)(2,1)S(1)} %constant_dynamic-slice_fusion), kind=kLoop, calls=%fused_computation.111 | loop fusion | flops 4194304 | bytes 1048580 | tf_op jit(solution)/shard_map/jit(_roll_dynamic)/concatenate | solution.py:60
  260.6 30.6 %all-reduce.1 = f32[32]{0:T(128)S(1)} all-reduce(f32[32]{0:T(128)S(1)} %convert_reduce_fusion), channel_id=3, replica_groups=mesh['groups'=2,'sec'=4,'plane'=4] {'sec','plane'}, use_global_device_ids=true, to_apply=%region_10.13.clone | all-reduce | flops 32 | bytes 256
  297.4 90.1 %all-reduce.4.cloned.1.call-done = f32[32,1024]{1,0:T(8,128)} async-done(((f32[32,1024]{1,0:T(8,128)}), f32[32,1024]{1,0:T(8,128)}) %all-reduce.4.cloned.1.call-update) | async-done | bytes 131088
  (179 shorter events, 86.0 us)
Async XLA Ops:
  30.4 12.7 %collective-permute-start.2 = (bf16[256,768]{1,0:T(8,128)(2,1)S(1)}, bf16[256,768]{1,0:T(8,128)(2,1)}, u32[]{:S(2)}, u32[]{:S(2)}) collective-permute-start(bf16[256,768]{1,0:T(8,128)(2,1)S(1)} %collective-permute-done.1), channel_id=1, source_target_pairs={{0,1},{1,2},{2,3},{3,0},{4,5},{5,6},{6,7},{7,4},{8,9},{9,10},{10,1... | collective-permute-start | bytes 1179656 | tf_op jit(solution)/shard_map/ppermute | solution.py:56
  32.0 33.8 %collective-permute-start.8 = (bf16[256,256]{1,0:T(8,128)(2,1)S(1)}, bf16[256,256]{1,0:T(8,128)(2,1)}, u32[]{:S(2)}, u32[]{:S(2)}) collective-permute-start(bf16[256,256]{1,0:T(8,128)(2,1)S(1)} %constant_dynamic-slice_fusion.2), channel_id=1, source_target_pairs={{0,1},{1,2},{2,3},{3,0},{4,5},{5,6},{6,7},{7,4},{8,9},{9,10},{10,1... | collective-permute-start | bytes 393224 | tf_op jit(solution)/shard_map/ppermute | solution.py:56
  53.3 32.8 %collective-permute-start.3 = (bf16[1024,768]{1,0:T(8,128)(2,1)S(1)}, bf16[1024,768]{1,0:T(8,128)(2,1)}, u32[]{:S(2)}, u32[]{:S(2)}) collective-permute-start(bf16[1024,768]{1,0:T(8,128)(2,1)S(1)} %fusion.28), channel_id=1, source_target_pairs={{0,16},{16,0},{1,17},{17,1},{2,18},{18,2},{3,19},{19,3},{4,20},{20... | collective-permute-start | bytes 4718600 | tf_op jit(solution)/shard_map/ppermute | solution.py:67
  65.7 13.0 %collective-permute-start.15 = (bf16[256,768]{1,0:T(8,128)(2,1)S(1)}, bf16[256,768]{1,0:T(8,128)(2,1)}, u32[]{:S(2)}, u32[]{:S(2)}) collective-permute-start(bf16[256,768]{1,0:T(8,128)(2,1)S(1)} %collective-permute-done.14), channel_id=1, source_target_pairs={{0,1},{1,2},{2,3},{3,0},{4,5},{5,6},{6,7},{7,4},{8,9},{9,10},{10,1... | collective-permute-start | bytes 1179656 | tf_op jit(solution)/shard_map/ppermute | solution.py:56
  65.8 12.9 %collective-permute-start.9 = (bf16[256,256]{1,0:T(8,128)(2,1)}, bf16[256,256]{1,0:T(8,128)(2,1)}, u32[]{:S(2)}, u32[]{:S(2)}) collective-permute-start(bf16[256,256]{1,0:T(8,128)(2,1)} %collective-permute-done.8), channel_id=1, source_target_pairs={{0,1},{1,2},{2,3},{3,0},{4,5},{5,6},{6,7},{7,4},{8,9},{9,10},{10,1... | collective-permute-start | bytes 393224 | tf_op jit(solution)/shard_map/ppermute | solution.py:56
  68.6 37.0 %collective-permute-start.4 = (bf16[1024,768]{1,0:T(8,128)(2,1)S(1)}, bf16[1024,768]{1,0:T(8,128)(2,1)}, u32[]{:S(2)}, u32[]{:S(2)}) collective-permute-start(bf16[1024,768]{1,0:T(8,128)(2,1)S(1)} %fusion.28), channel_id=1, source_target_pairs={{0,4},{4,0},{8,12},{12,8},{1,5},{5,1},{9,13},{13,9},{2,6},{6,2},{1... | collective-permute-start | bytes 4718600 | tf_op jit(solution)/shard_map/ppermute | solution.py:72
  78.7 13.2 %collective-permute-start.16 = (bf16[256,768]{1,0:T(8,128)(2,1)}, bf16[256,768]{1,0:T(8,128)(2,1)}, u32[]{:S(2)}, u32[]{:S(2)}) collective-permute-start(bf16[256,768]{1,0:T(8,128)(2,1)} %collective-permute-done.15), channel_id=1, source_target_pairs={{0,1},{1,2},{2,3},{3,0},{4,5},{5,6},{6,7},{7,4},{8,9},{9,10},{10,1... | collective-permute-start | bytes 1179656 | tf_op jit(solution)/shard_map/ppermute | solution.py:56
  86.1 21.5 %collective-permute-start.5 = (bf16[1024,768]{1,0:T(8,128)(2,1)}, bf16[1024,768]{1,0:T(8,128)(2,1)S(1)}, u32[]{:S(2)}, u32[]{:S(2)}) collective-permute-start(bf16[1024,768]{1,0:T(8,128)(2,1)} %collective-permute-done.3), channel_id=1, source_target_pairs={{0,4},{4,0},{8,12},{12,8},{1,5},{5,1},{9,13},{13,9},{2,6},{6,2},{1... | collective-permute-start | bytes 4718600 | tf_op jit(solution)/shard_map/ppermute | solution.py:72
  91.1 23.6 %collective-permute-start.11 = (bf16[1024,256]{1,0:T(8,128)(2,1)}, bf16[1024,256]{1,0:T(8,128)(2,1)}, u32[]{:S(2)}, u32[]{:S(2)}) collective-permute-start(bf16[1024,256]{1,0:T(8,128)(2,1)} %fusion.50), channel_id=1, source_target_pairs={{0,16},{16,0},{1,17},{17,1},{2,18},{18,2},{3,19},{19,3},{4,20},{20... | collective-permute-start | bytes 1572872 | tf_op jit(solution)/shard_map/ppermute | solution.py:67
  101.6 37.8 %collective-permute-start.17 = (bf16[1024,768]{1,0:T(8,128)(2,1)}, bf16[1024,768]{1,0:T(8,128)(2,1)}, u32[]{:S(2)}, u32[]{:S(2)}) collective-permute-start(bf16[1024,768]{1,0:T(8,128)(2,1)} %fusion.21), channel_id=1, source_target_pairs={{0,16},{16,0},{1,17},{17,1},{2,18},{18,2},{3,19},{19,3},{4,20},{20... | collective-permute-start | bytes 4718600 | tf_op jit(solution)/shard_map/ppermute | solution.py:67
  109.1 30.3 %collective-permute-start.6 = (bf16[128,2048]{1,0:T(8,128)(2,1)}, bf16[128,2048]{1,0:T(8,128)(2,1)}, u32[]{:S(2)}, u32[]{:S(2)}) collective-permute-start(bf16[128,2048]{1,0:T(8,128)(2,1)} %get-tuple-element.87), channel_id=1, source_target_pairs={{0,4},{4,8},{8,12},{1,5},{5,9},{9,13},{2,6},{6,10},{10,14},{3,7},{... | collective-permute-start | bytes 1572872 | tf_op jit(solution)/shard_map/ppermute | solution.py:17
  111.8 28.1 %collective-permute-start.7 = (bf16[128,2048]{1,0:T(8,128)(2,1)S(1)}, bf16[128,2048]{1,0:T(8,128)(2,1)}, u32[]{:S(2)}, u32[]{:S(2)}) collective-permute-start(bf16[128,2048]{1,0:T(8,128)(2,1)S(1)} %get-tuple-element.88), channel_id=1, source_target_pairs={{4,0},{8,4},{12,8},{5,1},{9,5},{13,9},{6,2},{10,6},{14,10},{7,3},{... | collective-permute-start | bytes 1572872 | tf_op jit(solution)/shard_map/ppermute | solution.py:17
  113.4 44.3 %collective-permute-start.12 = (bf16[1024,256]{1,0:T(8,128)(2,1)}, bf16[1024,256]{1,0:T(8,128)(2,1)}, u32[]{:S(2)}, u32[]{:S(2)}) collective-permute-start(bf16[1024,256]{1,0:T(8,128)(2,1)} %fusion.50), channel_id=1, source_target_pairs={{0,4},{4,0},{8,12},{12,8},{1,5},{5,1},{9,13},{13,9},{2,6},{6,2},{1... | collective-permute-start | bytes 1572872 | tf_op jit(solution)/shard_map/ppermute | solution.py:72
  114.6 44.5 %collective-permute-start.13 = (bf16[1024,256]{1,0:T(8,128)(2,1)}, bf16[1024,256]{1,0:T(8,128)(2,1)}, u32[]{:S(2)}, u32[]{:S(2)}) collective-permute-start(bf16[1024,256]{1,0:T(8,128)(2,1)} %collective-permute-done.11), channel_id=1, source_target_pairs={{0,4},{4,0},{8,12},{12,8},{1,5},{5,1},{9,13},{13,9},{2,6},{6,2},{1... | collective-permute-start | bytes 1572872 | tf_op jit(solution)/shard_map/ppermute | solution.py:72
  139.4 25.6 %collective-permute-start.18 = (bf16[1024,768]{1,0:T(8,128)(2,1)}, bf16[1024,768]{1,0:T(8,128)(2,1)}, u32[]{:S(2)}, u32[]{:S(2)}) collective-permute-start(bf16[1024,768]{1,0:T(8,128)(2,1)} %fusion.21), channel_id=1, source_target_pairs={{0,4},{4,0},{8,12},{12,8},{1,5},{5,1},{9,13},{13,9},{2,6},{6,2},{1... | collective-permute-start | bytes 4718600 | tf_op jit(solution)/shard_map/ppermute | solution.py:72
  139.4 27.7 %collective-permute-start.19 = (bf16[1024,768]{1,0:T(8,128)(2,1)}, bf16[1024,768]{1,0:T(8,128)(2,1)}, u32[]{:S(2)}, u32[]{:S(2)}) collective-permute-start(bf16[1024,768]{1,0:T(8,128)(2,1)} %collective-permute-done.17), channel_id=1, source_target_pairs={{0,4},{4,0},{8,12},{12,8},{1,5},{5,1},{9,13},{13,9},{2,6},{6,2},{1... | collective-permute-start | bytes 4718600 | tf_op jit(solution)/shard_map/ppermute | solution.py:72
  171.9 46.2 %all-to-all-start.1 = ((bf16[4,8,128,192]{2,3,1,0:T(8,128)(2,1)}), bf16[4,8,128,192]{2,3,1,0:T(8,128)(2,1)S(1)}, u32[]{:S(2)}, u32[]{:S(2)}) async-start(bf16[4,8,128,192]{2,3,1,0:T(8,128)(2,1)} %bitcast.26), calls=%async_computation.1 | async-start | bytes 3145728 | tf_op jit(solution)/shard_map/all_to_all | solution.py:185
  179.7 35.9 %collective-permute-start.20 = (bf16[256,256]{1,0:T(8,128)(2,1)S(1)}, bf16[256,256]{1,0:T(8,128)(2,1)S(1)}, u32[]{:S(2)}, u32[]{:S(2)}) collective-permute-start(bf16[256,256]{1,0:T(8,128)(2,1)S(1)} %constant_dynamic-slice_fusion), channel_id=1, source_target_pairs={{0,1},{1,2},{2,3},{3,0},{4,5},{5,6},{6,7},{7,4},{8,9},{9,10},{10,1... | collective-permute-start | bytes 393224 | tf_op jit(solution)/shard_map/ppermute | solution.py:56
  218.7 11.1 %all-to-all-start = ((bf16[4,8,128]{2,1,0:T(8,128)(2,1)}), bf16[4,8,128]{2,1,0:T(8,128)(2,1)S(1)}, u32[]{:S(2)}, u32[]{:S(2)}) async-start(bf16[4,8,128]{2,1,0:T(8,128)(2,1)} %broadcast_in_dim.86), calls=%async_computation | async-start | bytes 16384 | tf_op jit(solution)/shard_map/all_to_all | solution.py:186
  225.7 27.9 %collective-permute-start.22 = (bf16[256,256]{1,0:T(8,128)(2,1)S(1)}, bf16[256,256]{1,0:T(8,128)(2,1)S(1)}, u32[]{:S(2)}, u32[]{:S(2)}) collective-permute-start(bf16[256,256]{1,0:T(8,128)(2,1)S(1)} %collective-permute-done.21), channel_id=1, source_target_pairs={{0,1},{1,2},{2,3},{3,0},{4,5},{5,6},{6,7},{7,4},{8,9},{9,10},{10,1... | collective-permute-start | bytes 393224 | tf_op jit(solution)/shard_map/ppermute | solution.py:56
  248.8 42.5 %all-to-all-start.2 = ((bf16[4,2,32768]{2,1,0:T(2,128)(2,1)}), bf16[4,2,32768]{2,1,0:T(2,128)(2,1)S(1)}, u32[]{:S(2)}, u32[]{:S(2)}) async-start(bf16[4,2,32768]{2,1,0:T(2,128)(2,1)} %reshape.161), calls=%async_computation.2 | async-start | bytes 1048576 | tf_op jit(solution)/shard_map/all_to_all | solution.py:189
  253.6 133.9 %all-reduce.4.cloned.1.call-start = ((), (), s32[]{:S(2)}) async-start(), calls=%async_computation.3 | async-start | bytes 262144
  258.4 32.8 %collective-permute-start.23 = (bf16[1024,256]{1,0:T(8,128)(2,1)S(1)}, bf16[1024,256]{1,0:T(8,128)(2,1)S(1)}, u32[]{:S(2)}, u32[]{:S(2)}) collective-permute-start(bf16[1024,256]{1,0:T(8,128)(2,1)S(1)} %fusion.43), channel_id=1, source_target_pairs={{0,16},{16,0},{1,17},{17,1},{2,18},{18,2},{3,19},{19,3},{4,20},{20... | collective-permute-start | bytes 1572872 | tf_op jit(solution)/shard_map/ppermute | solution.py:67
  259.2 35.2 %collective-permute-start.24 = (bf16[1024,256]{1,0:T(8,128)(2,1)S(1)}, bf16[1024,256]{1,0:T(8,128)(2,1)S(1)}, u32[]{:S(2)}, u32[]{:S(2)}) collective-permute-start(bf16[1024,256]{1,0:T(8,128)(2,1)S(1)} %fusion.43), channel_id=1, source_target_pairs={{0,4},{4,0},{8,12},{12,8},{1,5},{5,1},{9,13},{13,9},{2,6},{6,2},{1... | collective-permute-start | bytes 1572872 | tf_op jit(solution)/shard_map/ppermute | solution.py:72
  (18 other events, 378.1 us)
Sparse Core Ops, SparseCore 0:
  297.4 90.0 all-reduce.3
